TPU v7x, 256 devices: a whole 4x4x8 slice. The times are simulated.
256 devices in a mesh: users: 64 (over y_lo, x, z), panel: 4 (over y_hi, core).
Axes of the slice: x: 4, y: 4 (y_hi: 2, y_lo: 2; y = y_hi * 2 + y_lo), z: 8, core: 2. Of those that a mesh axis runs over, the one named last changes fastest.
Arguments:
- user_emb0: float32 [65536, 128], P('users'), may hold values from -6 to 6
- item_base: float32 [4, 8192, 128], P('panel'), may hold values from -6 to 6
- weight_tiles: bfloat16 [64, 128, 128], replicated, may hold values from -0.02734375 to 0.02734375
- blk_user: int32 [64, 4, 384], P('users', 'panel'), may hold values from 0 to 7
- blk_item: int32 [64, 4, 384], P('users', 'panel'), may hold values from 0 to 63
- blk_weight: int32 [64, 4, 384], P('users', 'panel'), may hold values from 0 to 63
Outputs:
- user_out: float32 [65536, 128], P('users')
- item_emb: float32 [4, 8192, 128], P('panel', 'users')
All inputs are finite; a program needn't handle non-finite values.
Results may differ from a plain program's by a relative error of at most 0.0036.
Values may be sent and summed in bfloat16 or wider, within the bound.
No kernel may reach another device: no remote copies, remote signals or barrier semaphores. Data moves between devices by JAX's collectives and lax.ppermute only.
A program may use at most 128 MiB of HBM per device.

v0:
```python
import jax
import jax.numpy as jnp
from jax import lax
from jax.sharding import PartitionSpec as P

teleport = 0.2


def item_terms(user_tiles, users, items, weights, weight_tiles, n_items):
    group_size = min(users.shape[0], 128)
    pieces = (
        users.reshape(-1, group_size),
        items.reshape(-1, group_size),
        weights.reshape(-1, group_size),
    )

    def item_add_group(totals, lists):
        tiles = weight_tiles[lists[2]]
        rows = user_tiles[lists[0]]
        products = jnp.einsum("gab,gae->gbe", tiles, rows, preferred_element_type=jnp.float32)
        return (totals + jax.ops.segment_sum(products, lists[1], num_segments=n_items), None)

    start = jnp.zeros((n_items, user_tiles.shape[1], user_tiles.shape[2]), jnp.float32)
    totals, unused = lax.scan(item_add_group, start, pieces)
    return totals


def user_terms(item_tiles, users, items, weights, weight_tiles, n_tiles):
    group_size = min(users.shape[0], 128)
    pieces = (
        users.reshape(-1, group_size),
        items.reshape(-1, group_size),
        weights.reshape(-1, group_size),
    )

    def user_add_group(totals, lists):
        tiles = weight_tiles[lists[2]]
        rows = item_tiles[lists[1]]
        products = jnp.einsum("gab,gbe->gae", tiles, rows, preferred_element_type=jnp.float32)
        return (totals + jax.ops.segment_sum(products, lists[0], num_segments=n_tiles), None)

    start = jnp.zeros((n_tiles, item_tiles.shape[1], item_tiles.shape[2]), jnp.float32)
    totals, unused = lax.scan(user_add_group, start, pieces)
    return totals


def per_device(user_emb0, item_base, weight_tiles, blk_user, blk_item, blk_weight):
    tile_rows = weight_tiles.shape[1]
    width = user_emb0.shape[1]
    n_users = lax.axis_size("users")
    user_tiles = user_emb0.astype(jnp.bfloat16).reshape(-1, tile_rows, width)
    n_user_tiles = user_tiles.shape[0]
    user_list = blk_user.reshape(-1)
    item_list = blk_item.reshape(-1)
    weight_list = blk_weight.reshape(-1)
    partial_value = item_terms(user_tiles, user_list, item_list, weight_list, weight_tiles, n_users)
    partial_flat = partial_value.reshape(n_users * tile_rows, width)
    panel_base = item_base[0]
    position = lax.axis_index("users")
    totals = lax.psum(partial_flat, "users")
    panel_emb = (1.0 - teleport) * totals + teleport * panel_base
    own_emb = lax.dynamic_slice_in_dim(panel_emb, position * tile_rows, tile_rows, 0)
    panel_bf = panel_emb.astype(jnp.bfloat16)
    item_tiles = panel_bf.reshape(n_users, tile_rows, width)
    user_part = user_terms(
        item_tiles, user_list, item_list, weight_list, weight_tiles, n_user_tiles
    )
    user_sum = lax.psum(user_part, "panel")
    user_out = (1.0 - teleport) * user_sum.reshape(-1, width) + teleport * user_emb0
    return (user_out, own_emb[None])


def solution(mesh):
    placed = (
        P("users", None),
        P("panel", None, None),
        P(),
        P("users", "panel", None),
        P("users", "panel", None),
        P("users", "panel", None),
    )
    return jax.shard_map(
        per_device,
        mesh=mesh,
        in_specs=placed,
        out_specs=(P("users", None), P("panel", "users", None)),
        check_vma=False,
    )
```

profile of v0, /device:TPU:1, one launch (start us, length us, event | category | flops | bytes accessed | tf_op | source)
XLA Modules:
  0.0 918.1 jit_solution(14164029038932604751)
XLA Ops:
  7.2 0.0 copy-start.1
  7.2 0.0 all-reduce.3.cloned.1.call-start
  7.2 0.8 reduce
  8.1 0.7 reduce.1
  8.8 0.7 reduce.2
  9.5 1.1 convert_element_type.6
  10.5 2.4 broadcast.84
  13.0 0.0 copy-done.1
  13.0 121.0 %while.20 = (s32[]{:T(128)}, f32[64,128,128]{2,1,0:T(8,128)}, s32[3,128]{1,0:T(4,128)S(1)}, s32[3,128]{1,0:T(4,128)S(1)}, bf16[64,128,128]{2,1,0:T(8,128)(2,1)S(...) while((s32[]{:T(128)}, f32[64,128,128]{2,1,0:T(8,128)}, ...), condition=%wide.region_2.3_spmd, body=%wide.region_0.2_spmd.sunk | while | flops 538970880 | bytes 58734172 | solution.py:24
  13.0 3.1 gather_fusion
  16.1 3.0 gather_fusion.1
  19.1 8.2 fusion.31
  27.3 25.9 %scatter_fusion = f32[64,128,128]{2,1,0:T(8,128)} fusion(f32[64,128,128]{2,1,0:T(8,128)} %get-tuple-element.215, s32[128]{0:T(128)S(1)} %fusion.29, f32[128,128,128]{2,1,0:T(8,128)} %fusion.31), kind=kCustom, calls=%fused_computation.4.clone.1 | custom fusion | flops 2097152 | bytes 25166336 | tf_op jit(solution)/shard_map/while/body/eval_jaxpr/scatter-add | solution.py:21
  53.2 3.1 gather_fusion
  56.3 3.0 gather_fusion.1
  59.3 8.2 fusion.31
  67.5 26.0 %scatter_fusion = f32[64,128,128]{2,1,0:T(8,128)} fusion(f32[64,128,128]{2,1,0:T(8,128)} %get-tuple-element.215, s32[128]{0:T(128)S(1)} %fusion.29, f32[128,128,128]{2,1,0:T(8,128)} %fusion.31), kind=kCustom, calls=%fused_computation.4.clone.1 | custom fusion | flops 2097152 | bytes 25166336 | tf_op jit(solution)/shard_map/while/body/eval_jaxpr/scatter-add | solution.py:21
  93.5 3.1 gather_fusion
  96.6 3.0 gather_fusion.1
  99.6 8.2 fusion.31
  107.9 26.1 %scatter_fusion = f32[64,128,128]{2,1,0:T(8,128)} fusion(f32[64,128,128]{2,1,0:T(8,128)} %get-tuple-element.215, s32[128]{0:T(128)S(1)} %fusion.29, f32[128,128,128]{2,1,0:T(8,128)} %fusion.31), kind=kCustom, calls=%fused_computation.4.clone.1 | custom fusion | flops 2097152 | bytes 25166336 | tf_op jit(solution)/shard_map/while/body/eval_jaxpr/scatter-add | solution.py:21
  134.0 0.0 all-reduce.3.cloned.1.call-update
  134.0 0.0 all-reduce.5.cloned.1.call-start
  134.1 576.4 %all-reduce.3.cloned.1.call-done = f32[8192,128]{1,0:T(8,128)} async-done(((f32[8192,128]{1,0:T(8,128)}), f32[8192,128]{1,0:T(8,128)}) %all-reduce.3.cloned.1.call-update) | async-done | bytes 4194320 | tf_op jit(solution)/shard_map/psum | solution.py:60
  710.5 7.0 fusion.10
  717.5 0.0 copy-start.2
  717.5 98.0 %while.21 = (s32[]{:T(128)}, f32[8,128,128]{2,1,0:T(8,128)S(1)}, s32[3,128]{1,0:T(4,128)S(1)}, s32[3,128]{1,0:T(4,128)S(1)}, bf16[64,128,128]{2,1,0:T(8,128)(2,1...) while((s32[]{:T(128)}, f32[8,128,128]{2,1,0:T(8,128)S(1)}, ...), condition=%wide.region_6.7_spmd, body=%wide.region_4.6_spmd.sunk | while | flops 538970880 | bytes 58734172 | solution.py:43
  717.5 3.0 gather_fusion.2
  720.6 4.6 gather_fusion.3
  725.2 7.9 fusion.36
  733.1 17.0 %scatter_fusion.1 = f32[8,128,128]{2,1,0:T(8,128)S(1)} fusion(f32[8,128,128]{2,1,0:T(8,128)S(1)} %get-tuple-element.239, s32[128]{0:T(128)S(1)} %fusion.34, f32[128,128,128]{2,1,0:T(8,128)} %fusion.36), kind=kCustom, calls=%fused_computation.5.clone.1 | custom fusion | flops 2097152 | bytes 25166336 | tf_op jit(solution)/shard_map/while/body/eval_jaxpr/scatter-add | solution.py:40
  750.2 3.0 gather_fusion.2
  753.3 4.6 gather_fusion.3
  757.9 7.9 fusion.36
  765.8 17.0 %scatter_fusion.1 = f32[8,128,128]{2,1,0:T(8,128)S(1)} fusion(f32[8,128,128]{2,1,0:T(8,128)S(1)} %get-tuple-element.239, s32[128]{0:T(128)S(1)} %fusion.34, f32[128,128,128]{2,1,0:T(8,128)} %fusion.36), kind=kCustom, calls=%fused_computation.5.clone.1 | custom fusion | flops 2097152 | bytes 25166336 | tf_op jit(solution)/shard_map/while/body/eval_jaxpr/scatter-add | solution.py:40
  782.9 3.0 gather_fusion.2
  785.9 4.6 gather_fusion.3
  790.5 7.9 fusion.36
  798.5 17.0 %scatter_fusion.1 = f32[8,128,128]{2,1,0:T(8,128)S(1)} fusion(f32[8,128,128]{2,1,0:T(8,128)S(1)} %get-tuple-element.239, s32[128]{0:T(128)S(1)} %fusion.34, f32[128,128,128]{2,1,0:T(8,128)} %fusion.36), kind=kCustom, calls=%fused_computation.5.clone.1 | custom fusion | flops 2097152 | bytes 25166336 | tf_op jit(solution)/shard_map/while/body/eval_jaxpr/scatter-add | solution.py:40
  815.5 0.0 copy-start
  815.5 0.8 copy-done
  816.3 0.0 all-reduce.5.cloned.1.call-update
  816.3 1.5 dynamic-slice_bitcast_fusion
  817.8 91.5 %all-reduce.5.cloned.1.call-done = f32[8,128,128]{2,1,0:T(8,128)} async-done(((f32[8,128,128]{2,1,0:T(8,128)}), f32[8,128,128]{2,1,0:T(8,128)}) %all-reduce.5.cloned.1.call-update) | async-done | bytes 524304 | tf_op jit(solution)/shard_map/psum | solution.py:68
  909.3 1.1 broadcast_multiply_fusion
  910.4 0.0 copy-done.2
  910.4 0.9 bitcast_add_fusion.1
  (25 shorter events, 0.2 us)
Async XLA Ops:
  7.2 5.8 copy-start.1
  7.2 703.3 %all-reduce.3.cloned.1.call-start = ((), (), s32[]{:S(2)}) async-start(), calls=%async_computation | async-start | bytes 8388608 | tf_op jit(solution)/shard_map/psum | solution.py:60
  134.0 775.3 %all-reduce.5.cloned.1.call-start = ((), (), s32[]{:S(2)}) async-start(), calls=%async_computation.1 | async-start | bytes 1048576 | tf_op jit(solution)/shard_map/psum | solution.py:68
  717.5 192.9 %copy-start.2 = (f32[1024,128]{1,0:T(8,128)S(1)}, f32[1024,128]{1,0:T(8,128)}, u32[]{:S(2)}) copy-start(f32[1024,128]{1,0:T(8,128)} %param.10) | copy-start | bytes 1572868
  815.5 0.8 copy-start
Sparse Core Ops, SparseCore 0:
  134.1 576.2 all-reduce.2
  816.4 92.7 all-reduce.4
where the time goes:
time: 920 us; the launch traced here: 918 us
  waiting for transfers between devices  668 us (73%)
  other arithmetic  141 us (15%)
  matrix products  48.5 us (5%)
  local copies, waits for them, and re-layouts  46 us (5%)
  between operations  14.1 us (2%)
    psum x1, waiting for transfers between devices, per_device(): totals = lax.psum(partial_flat, 'users')  576 us
    psum x1, waiting for transfers between devices, per_device(): user_sum = lax.psum(user_part, 'panel')  91.5 us
    scatter-add x3, other arithmetic, item_add_group(): jax.ops.segment_sum(products, lists[1], num_segments=n_items)  78 us
    scatter-add x3, other arithmetic, user_add_group(): jax.ops.segment_sum(products, lists[0], num_segments=n_tiles)  51.1 us
    dot_general x3, matrix products, item_add_group(): jnp.einsum('gab,gae->gbe', tiles, rows, preferred_element_type=jnp.float32)  24.7 us
    dot_general x3, matrix products, user_add_group(): jnp.einsum('gab,gbe->gae', tiles, rows, preferred_element_type=jnp.float32)  23.8 us
  transfers between devices with their start and end apart: 2, of which 2 were waited for; matrix products, arithmetic and copies ran while one was open for 0% of the time, Pallas kernels for 0%

commit v1 on v0

--- a/solution.py
+++ b/solution.py
@@ -65,7 +65,7 @@
     user_part = user_terms(
         item_tiles, user_list, item_list, weight_list, weight_tiles, n_user_tiles
     )
-    user_sum = lax.psum(user_part, "panel")
+    user_sum = jnp.sum(lax.all_gather(user_part, "panel"), axis=0)
     user_out = (1.0 - teleport) * user_sum.reshape(-1, width) + teleport * user_emb0
     return (user_out, own_emb[None])
 

time: 920 us -> 902 us (0.980)
  waiting for transfers between devices: 668 us -> 649 us
    psum x1 -> x0, waiting for transfers between devices: 91.5 us -> none  [per_device(): user_sum = lax.psum(user_part, 'panel')]
    all_gather x0 -> x1, waiting for transfers between devices: none -> 73 us  [per_device(): user_sum = jnp.sum(lax.all_gather(user_part, 'panel'), axis=0)]
where the time goes in v1:
time: 902 us; the launch traced here: 900 us
  waiting for transfers between devices  649 us (72%)
  other arithmetic  142 us (16%)
  matrix products  48.5 us (5%)
  local copies, waits for them, and re-layouts  46 us (5%)
  between operations  14.1 us (2%)
    psum x1, waiting for transfers between devices, per_device(): totals = lax.psum(partial_flat, 'users')  576 us
    scatter-add x3, other arithmetic, item_add_group(): jax.ops.segment_sum(products, lists[1], num_segments=n_items)  78 us
    all_gather x1, waiting for transfers between devices, per_device(): user_sum = jnp.sum(lax.all_gather(user_part, 'panel'), axis=0)  73 us
    scatter-add x3, other arithmetic, user_add_group(): jax.ops.segment_sum(products, lists[0], num_segments=n_tiles)  51.1 us
    dot_general x3, matrix products, item_add_group(): jnp.einsum('gab,gae->gbe', tiles, rows, preferred_element_type=jnp.float32)  24.7 us
    dot_general x3, matrix products, user_add_group(): jnp.einsum('gab,gbe->gae', tiles, rows, preferred_element_type=jnp.float32)  23.8 us
  transfers between devices with their start and end apart: 2, of which 2 were waited for; matrix products, arithmetic and copies ran while one was open for 0% of the time, Pallas kernels for 0%

profile of v1, /device:TPU:1, one launch (start us, length us, event | category | flops | bytes accessed | tf_op | source)
XLA Modules:
  0.0 900.3 jit_solution(7347126226761411298)
XLA Ops:
  7.2 0.0 copy-start.1
  7.2 0.0 all-reduce.2.cloned.1.call-start
  7.2 0.8 reduce
  8.1 0.7 reduce.1
  8.8 0.7 reduce.2
  9.5 1.1 convert_element_type.6
  10.5 2.4 broadcast.84
  13.0 0.0 copy-done.1
  13.0 121.0 %while.20 = (s32[]{:T(128)}, f32[64,128,128]{2,1,0:T(8,128)}, s32[3,128]{1,0:T(4,128)S(1)}, s32[3,128]{1,0:T(4,128)S(1)}, bf16[64,128,128]{2,1,0:T(8,128)(2,1)S(...) while((s32[]{:T(128)}, f32[64,128,128]{2,1,0:T(8,128)}, ...), condition=%wide.region_2.3_spmd, body=%wide.region_0.2_spmd.sunk | while | flops 538970880 | bytes 58734172 | solution.py:24
  13.0 3.1 gather_fusion
  16.1 3.0 gather_fusion.1
  19.1 8.2 fusion.31
  27.3 25.9 %scatter_fusion = f32[64,128,128]{2,1,0:T(8,128)} fusion(f32[64,128,128]{2,1,0:T(8,128)} %get-tuple-element.215, s32[128]{0:T(128)S(1)} %fusion.29, f32[128,128,128]{2,1,0:T(8,128)} %fusion.31), kind=kCustom, calls=%fused_computation.4.clone.1 | custom fusion | flops 2097152 | bytes 25166336 | tf_op jit(solution)/shard_map/while/body/eval_jaxpr/scatter-add | solution.py:21
  53.2 3.1 gather_fusion
  56.3 3.0 gather_fusion.1
  59.3 8.2 fusion.31
  67.5 26.0 %scatter_fusion = f32[64,128,128]{2,1,0:T(8,128)} fusion(f32[64,128,128]{2,1,0:T(8,128)} %get-tuple-element.215, s32[128]{0:T(128)S(1)} %fusion.29, f32[128,128,128]{2,1,0:T(8,128)} %fusion.31), kind=kCustom, calls=%fused_computation.4.clone.1 | custom fusion | flops 2097152 | bytes 25166336 | tf_op jit(solution)/shard_map/while/body/eval_jaxpr/scatter-add | solution.py:21
  93.5 3.1 gather_fusion
  96.6 3.0 gather_fusion.1
  99.6 8.2 fusion.31
  107.9 26.1 %scatter_fusion = f32[64,128,128]{2,1,0:T(8,128)} fusion(f32[64,128,128]{2,1,0:T(8,128)} %get-tuple-element.215, s32[128]{0:T(128)S(1)} %fusion.29, f32[128,128,128]{2,1,0:T(8,128)} %fusion.31), kind=kCustom, calls=%fused_computation.4.clone.1 | custom fusion | flops 2097152 | bytes 25166336 | tf_op jit(solution)/shard_map/while/body/eval_jaxpr/scatter-add | solution.py:21
  134.0 0.0 all-reduce.2.cloned.1.call-update
  134.0 0.0 all-gather.3.cloned.1.call-start
  134.1 576.4 %all-reduce.2.cloned.1.call-done = f32[8192,128]{1,0:T(8,128)} async-done(((f32[8192,128]{1,0:T(8,128)}), f32[8192,128]{1,0:T(8,128)}) %all-reduce.2.cloned.1.call-update) | async-done | bytes 4194320 | tf_op jit(solution)/shard_map/psum | solution.py:60
  710.5 7.0 fusion.10
  717.5 98.0 %while.21 = (s32[]{:T(128)}, f32[8,128,128]{2,1,0:T(8,128)S(1)}, s32[3,128]{1,0:T(4,128)S(1)}, s32[3,128]{1,0:T(4,128)S(1)}, bf16[64,128,128]{2,1,0:T(8,128)(2,1...) while((s32[]{:T(128)}, f32[8,128,128]{2,1,0:T(8,128)S(1)}, ...), condition=%wide.region_6.7_spmd, body=%wide.region_4.6_spmd.sunk | while | flops 538970880 | bytes 58734172 | solution.py:43
  717.5 3.0 gather_fusion.2
  720.6 4.6 gather_fusion.3
  725.2 7.9 fusion.36
  733.1 17.0 %scatter_fusion.1 = f32[8,128,128]{2,1,0:T(8,128)S(1)} fusion(f32[8,128,128]{2,1,0:T(8,128)S(1)} %get-tuple-element.239, s32[128]{0:T(128)S(1)} %fusion.34, f32[128,128,128]{2,1,0:T(8,128)} %fusion.36), kind=kCustom, calls=%fused_computation.5.clone.1 | custom fusion | flops 2097152 | bytes 25166336 | tf_op jit(solution)/shard_map/while/body/eval_jaxpr/scatter-add | solution.py:40
  750.2 3.0 gather_fusion.2
  753.3 4.6 gather_fusion.3
  757.8 7.9 fusion.36
  765.8 17.0 %scatter_fusion.1 = f32[8,128,128]{2,1,0:T(8,128)S(1)} fusion(f32[8,128,128]{2,1,0:T(8,128)S(1)} %get-tuple-element.239, s32[128]{0:T(128)S(1)} %fusion.34, f32[128,128,128]{2,1,0:T(8,128)} %fusion.36), kind=kCustom, calls=%fused_computation.5.clone.1 | custom fusion | flops 2097152 | bytes 25166336 | tf_op jit(solution)/shard_map/while/body/eval_jaxpr/scatter-add | solution.py:40
  782.9 3.0 gather_fusion.2
  785.9 4.6 gather_fusion.3
  790.5 7.9 fusion.36
  798.5 17.0 %scatter_fusion.1 = f32[8,128,128]{2,1,0:T(8,128)S(1)} fusion(f32[8,128,128]{2,1,0:T(8,128)S(1)} %get-tuple-element.239, s32[128]{0:T(128)S(1)} %fusion.34, f32[128,128,128]{2,1,0:T(8,128)} %fusion.36), kind=kCustom, calls=%fused_computation.5.clone.1 | custom fusion | flops 2097152 | bytes 25166336 | tf_op jit(solution)/shard_map/while/body/eval_jaxpr/scatter-add | solution.py:40
  815.5 0.0 copy-start
  815.5 0.0 copy-start.2
  815.5 0.8 copy-done
  816.3 0.0 all-gather.3.cloned.1.call-update
  816.3 1.5 dynamic-slice_bitcast_fusion
  817.8 73.0 %all-gather.3.cloned.1.call-done = f32[32,128,128]{2,1,0:T(8,128)} async-done(((f32[8,128,128]{2,1,0:T(8,128)}), f32[32,128,128]{2,1,0:T(8,128)}) %all-gather.3.cloned.1.call-update) | async-done | bytes 2097168 | tf_op jit(solution)/shard_map/all_gather | solution.py:68
  890.8 1.8 reduce_sum.9
  892.6 0.0 copy-done.2
  892.6 0.9 bitcast_add_fusion.1
  (26 shorter events, 0.2 us)
Async XLA Ops:
  7.2 5.8 copy-start.1
  7.2 703.3 %all-reduce.2.cloned.1.call-start = ((), (), s32[]{:S(2)}) async-start(), calls=%async_computation | async-start | bytes 8388608 | tf_op jit(solution)/shard_map/psum | solution.py:60
  134.0 756.7 %all-gather.3.cloned.1.call-start = ((), (), s32[]{:S(2)}) async-start(), calls=%async_computation.1 | async-start | bytes 2621440 | tf_op jit(solution)/shard_map/all_gather | solution.py:68
  815.5 0.8 copy-start
  815.5 77.1 %copy-start.2 = (f32[1024,128]{1,0:T(8,128)S(1)}, f32[1024,128]{1,0:T(8,128)}, u32[]{:S(2)}) copy-start(f32[1024,128]{1,0:T(8,128)} %param.10) | copy-start | bytes 1572868
Sparse Core Ops, SparseCore 0:
  134.1 576.2 all-reduce.1
  816.4 74.2 all-gather.2
